TPU v7x, 128 devices: a whole 4x4x4 slice. The times are simulated.
128 devices in a mesh: gx: 16 (over z, x), gy: 8 (over y, core).
Axes of the slice: x: 4, y: 4, z: 4, core: 2. Of those that a mesh axis runs over, the one named last changes fastest.
Arguments:
- tokens: bfloat16 [2048, 8192], P('gy', 'gx'), may hold values from -6 to 6
- gate_base_weight: bfloat16 [8192, 29568], P('gx', 'gy'), may hold values from -0.0625 to 0.0625
- up_base_weight: bfloat16 [8192, 29568], P('gx', 'gy'), may hold values from -0.0625 to 0.0625
- adapter_down_maps: bfloat16 [128, 8192, 128], P(('gx', 'gy')), may hold values from -0.0625 to 0.0625
- adapter_up_maps: bfloat16 [128, 128, 29568], P(('gx', 'gy')), may hold values from -0.75 to 0.75
- tenant: int32 [2048, 1], replicated, may hold values from 0 to 127; in each aligned block of 128 rows (0 to 127, 128 to 255, ...) at most 4 rows name the same one
- tenant_slot_index: int32 [128], replicated, may hold values from 0 to 127, as said below
Outputs:
- hidden: bfloat16 [2048, 29568], P('gx', 'gy')
Inputs may be any that keep to these rules, and one draw needn't show every extreme that they name: In each aligned block of 128 rows no tenant names more than 4 rows, and in some block a tenant names exactly 4. `tenant_slot_index`: A permutation of the slots; slot s is held by device s of gx+gy, gx the slower index.
All inputs are finite; a program needn't handle non-finite values.
Results may differ from a plain program's by a relative error of at most 0.019.
Values may be sent and summed in bfloat16 or wider, within the bound.
No kernel may reach another device: no remote copies, remote signals or barrier semaphores. Data moves between devices by JAX's collectives and lax.ppermute only.
A program may use at most 192 MiB of HBM per device.

v0:
```python
import jax
import jax.numpy as jnp
from jax import lax
from jax.sharding import PartitionSpec as P

CAP = 4


def body(
    tokens,
    gate_base_weight,
    up_base_weight,
    adapter_down_maps,
    adapter_up_maps,
    tenant,
    tenant_slot_index,
):
    tile_grid_rows = lax.axis_size("gx")
    tile_grid_columns = lax.axis_size("gy")
    devices = tile_grid_rows * tile_grid_columns
    row_gx = lax.axis_index("gx")
    row_gy = lax.axis_index("gy")
    local_rows = tokens.shape[0]
    tile_width = tokens.shape[1]
    total_rows = tenant.shape[0]
    block = total_rows // tile_grid_rows
    groups = local_rows // block
    tenants = tenant_slot_index.shape[0]
    column_count = gate_base_weight.shape[1]
    doubled_rank = adapter_down_maps.shape[2]
    adapter_rank_width = doubled_rank // 2
    gathered = lax.all_gather(tokens, "gy", axis=0, tiled=True)
    summed = lax.psum_scatter(
        jnp.concatenate(
            [
                jnp.dot(gathered, gate_base_weight, preferred_element_type=jnp.float32),
                jnp.dot(gathered, up_base_weight, preferred_element_type=jnp.float32),
            ],
            axis=1,
        ).astype(jnp.bfloat16),
        "gx",
        scatter_dimension=0,
        tiled=True,
    ).astype(jnp.float32)
    slot_all = jnp.sum(
        jnp.where(tenant == lax.iota(jnp.int32, tenants)[None, :], tenant_slot_index[None, :], 0),
        axis=1,
    )
    onehot = (slot_all[:, None] == lax.iota(jnp.int32, devices)[None, :]).astype(jnp.int32)
    blocked = onehot.reshape(tile_grid_rows, block, devices)
    before = jnp.cumsum(blocked, axis=1) - blocked
    position = jnp.sum(before * blocked, axis=2).reshape(total_rows)
    send_slot = lax.dynamic_slice_in_dim(slot_all, row_gy * local_rows, local_rows)
    send_rank = lax.dynamic_slice_in_dim(position, row_gy * local_rows, local_rows)
    target = (send_slot * groups + lax.iota(jnp.int32, local_rows) // block) * CAP + send_rank
    outgoing = jnp.zeros((devices * groups * CAP, tile_width), jnp.bfloat16).at[target].set(tokens)
    arrived = lax.all_to_all(
        outgoing.reshape(devices, groups * CAP, tile_width),
        ("gx", "gy"),
        split_axis=0,
        concat_axis=0,
        tiled=True,
    )
    arrived = arrived.reshape(tile_grid_rows, tile_grid_columns * groups * CAP, tile_width)
    down_local = adapter_down_maps[0].reshape(tile_grid_rows, tile_width, doubled_rank)
    low = jnp.einsum("isk,ikr->sr", arrived, down_local, preferred_element_type=jnp.float32).astype(
        jnp.bfloat16
    )
    low = low.reshape(tile_grid_rows, CAP, doubled_rank)
    gate_up_map = adapter_up_maps[0, :adapter_rank_width].reshape(
        adapter_rank_width, tile_grid_columns, column_count
    )
    up_up_map = adapter_up_maps[0, adapter_rank_width:].reshape(
        adapter_rank_width, tile_grid_columns, column_count
    )
    delta_gate = jnp.einsum(
        "gcr,rjf->gjcf",
        low[:, :, :adapter_rank_width],
        gate_up_map,
        preferred_element_type=jnp.float32,
    ).astype(jnp.bfloat16)
    delta_up = jnp.einsum(
        "gcr,rjf->gjcf",
        low[:, :, adapter_rank_width:],
        up_up_map,
        preferred_element_type=jnp.float32,
    ).astype(jnp.bfloat16)
    back_gate, back_up = (
        lax.all_to_all(
            delta_gate.reshape(devices, CAP, column_count),
            ("gx", "gy"),
            split_axis=0,
            concat_axis=0,
            tiled=True,
        ),
        lax.all_to_all(
            delta_up.reshape(devices, CAP, column_count),
            ("gx", "gy"),
            split_axis=0,
            concat_axis=0,
            tiled=True,
        ),
    )
    back_gate = back_gate.reshape(devices * CAP, column_count)
    back_up = back_up.reshape(devices * CAP, column_count)
    own_slot = lax.dynamic_slice_in_dim(slot_all, row_gx * block, block)
    own_rank = lax.dynamic_slice_in_dim(position, row_gx * block, block)
    pick = own_slot * CAP + own_rank
    gate_value = summed[:, :column_count] + back_gate[pick].astype(jnp.float32)
    up_value = summed[:, column_count:] + back_up[pick].astype(jnp.float32)
    return (jax.nn.silu(gate_value) * up_value).astype(jnp.bfloat16)


def solution(mesh):
    return jax.shard_map(
        body,
        mesh=mesh,
        in_specs=(
            P("gy", "gx"),
            P("gx", "gy"),
            P("gx", "gy"),
            P(("gx", "gy"), None, None),
            P(("gx", "gy"), None, None),
            P(),
            P(),
        ),
        out_specs=P("gx", "gy"),
        check_vma=False,
    )
```

profile of v0, /device:TPU:1, one launch (start us, length us, event | category | flops | bytes accessed | tf_op | source)
XLA Modules:
  0.0 404.3 jit_solution(10806545864353587675)
XLA Ops:
  7.3 30.6 %all-gather.2.cloned.1.call-done = bf16[2048,512]{1,0:T(8,128)(2,1)} async-done(((bf16[256,512]{1,0:T(8,128)(2,1)}), bf16[2048,512]{1,0:T(8,128)(2,1)}) %all-gather.2.cloned.1.call-update) | async-done | bytes 2097168 | tf_op jit(solution)/shard_map/all_gather | solution.py:32
  37.9 13.8 %convolution_convert_fusion = bf16[2048,3696]{0,1:T(8,128)(2,1)} fusion(bf16[2048,512]{1,0:T(8,128)(2,1)} %all-gather.2.cloned.1.call-done, bf16[512,3696]{0,1:T(8,128)(2,1)} %param.9), kind=kOutput, calls=%fused_computation.4 | convolution fusion | flops 7758643200 | bytes 21020672 | tf_op jit(solution)/shard_map/dot_general | solution.py:37
  51.8 10.8 %convolution_convert_fusion.1 = bf16[2048,3696]{0,1:T(8,128)(2,1)} fusion(bf16[2048,512]{1,0:T(8,128)(2,1)S(1)} %copy-done.6, bf16[512,3696]{0,1:T(8,128)(2,1)S(1)} %copy-done.5), kind=kOutput, calls=%fused_computation.5 | convolution fusion | flops 7758643200 | bytes 21020672 | tf_op jit(solution)/shard_map/dot_general | solution.py:36
  62.6 21.4 %pad_maximum_fusion = bf16[2048,7392]{0,1:T(8,128)(2,1)} fusion(bf16[2048,3696]{0,1:T(8,128)(2,1)} %convolution_convert_fusion, bf16[2048,3696]{0,1:T(8,128)(2,1)} %convolution_convert_fusion.1), kind=kLoop, calls=%fused_computation.3 | loop fusion | flops 60555264 | bytes 60555264 | tf_op jit(solution)/shard_map/concatenate | solution.py:34
  84.0 36.5 %copy.60 = bf16[2048,7392]{1,0:T(8,128)(2,1)} copy(bf16[2048,7392]{0,1:T(8,128)(2,1)} %pad_maximum_fusion) | data formatting | bytes 60555264
  124.9 3.1 scatter_custom_fusion
  127.9 8.1 %all-to-all-start = ((bf16[128,8,512]{2,1,0:T(8,128)(2,1)}), bf16[128,8,512]{2,1,0:T(8,128)(2,1)S(1)}, u32[]{:S(2)}, u32[]{:S(2)}) async-start(bf16[128,8,512]{2,1,0:T(8,128)(2,1)} %bitcast.48), calls=%async_computation | async-start | bytes 2097152 | tf_op jit(solution)/shard_map/all_to_all | solution.py:57
  136.1 5.6 %fusion.19 = (bf16[1,64,29568]{2,1,0:T(8,128)(2,1)}, bf16[1,64,29568]{2,1,0:T(8,128)(2,1)}) fusion(bf16[1,128,29568]{2,1,0:T(8,128)(2,1)} %param.11), kind=kLoop, calls=%fused_computation.44 | loop fusion | bytes 15138816 | tf_op jit(solution)/shard_map/slice | solution.py:70
  141.7 7.5 %reshape_squeeze.11 = bf16[64,8,3696]{2,1,0:T(8,128)(2,1)} reshape(bf16[1,64,29568]{2,1,0:T(8,128)(2,1)} %get-tuple-element.6) | data formatting | bytes 7569408 | tf_op jit(solution)/shard_map/reshape;squeeze | solution.py:73
  149.2 17.1 %all-to-all-done = bf16[128,8,512]{2,1,0:T(8,128)(2,1)S(1)} async-done(((bf16[128,8,512]{2,1,0:T(8,128)(2,1)}), bf16[128,8,512]{2,1,0:T(8,128)(2,1)S(1)}, u32[]{:S(2)}, u32[]{:S(2)}) %all-to-all-start) | async-done | bytes 1048608 | tf_op jit(solution)/shard_map/all_to_all | solution.py:57
  166.9 3.3 fusion.1
  170.9 4.9 %copy.56 = bf16[128,4,3696]{2,1,0:T(4,128)(2,1)} copy(bf16[128,4,3696]{2,0,1:T(8,128)(2,1)S(1)} %bitcast.45) | data formatting | bytes 7569408 | tf_op jit(solution)/shard_map/reshape | solution.py:97
  175.8 6.1 %all-to-all-start.2 = ((bf16[128,4,3696]{2,1,0:T(4,128)(2,1)}), bf16[128,4,3696]{2,1,0:T(4,128)(2,1)}, u32[]{:S(2)}, u32[]{:S(2)}) async-start(bf16[128,4,3696]{2,1,0:T(4,128)(2,1)} %copy.56), calls=%async_computation.2 | async-start | bytes 7602176 | tf_op jit(solution)/shard_map/all_to_all | solution.py:96
  181.9 7.5 %reshape_squeeze.10 = bf16[64,8,3696]{2,1,0:T(8,128)(2,1)} reshape(bf16[1,64,29568]{2,1,0:T(8,128)(2,1)} %get-tuple-element.5) | data formatting | bytes 7569408 | tf_op jit(solution)/shard_map/reshape;squeeze | solution.py:70
  189.4 3.2 fusion
  193.3 4.8 %copy.52 = bf16[128,4,3696]{2,1,0:T(4,128)(2,1)} copy(bf16[128,4,3696]{2,0,1:T(8,128)(2,1)S(1)} %bitcast.46) | data formatting | bytes 7569408 | tf_op jit(solution)/shard_map/reshape | solution.py:90
  198.0 65.6 %all-to-all-done.2 = bf16[128,4,3696]{2,1,0:T(4,128)(2,1)} async-done(((bf16[128,4,3696]{2,1,0:T(4,128)(2,1)}), bf16[128,4,3696]{2,1,0:T(4,128)(2,1)}, u32[]{:S(2)}, u32[]{:S(2)}) %all-to-all-start.2) | async-done | bytes 3784736 | tf_op jit(solution)/shard_map/all_to_all | solution.py:96
  263.6 6.3 %all-to-all-start.1 = ((bf16[128,4,3696]{2,1,0:T(4,128)(2,1)}), bf16[128,4,3696]{2,1,0:T(4,128)(2,1)}, u32[]{:S(2)}, u32[]{:S(2)}) async-start(bf16[128,4,3696]{2,1,0:T(4,128)(2,1)} %copy.52), calls=%async_computation.1 | async-start | bytes 7602176 | tf_op jit(solution)/shard_map/all_to_all | solution.py:89
  270.0 7.2 %reshape.42 = bf16[512,3696]{1,0:T(8,128)(2,1)} reshape(bf16[128,4,3696]{2,1,0:T(4,128)(2,1)} %all-to-all-done.2) | data formatting | bytes 7569408 | tf_op jit(solution)/shard_map/reshape | solution.py:105
  277.2 5.8 %gather_fusion.1 = bf16[128,3696]{1,0:T(8,128)(2,1)} fusion(bf16[512,3696]{1,0:T(8,128)(2,1)} %reshape.42, s32[1024]{0:T(1024)S(1)} %pad_clamp_fusion), kind=kCustom, calls=%fused_computation.1 | custom fusion | bytes 1892864 | tf_op jit(solution)/shard_map/gather | solution.py:110
  283.0 68.3 %all-to-all-done.1 = bf16[128,4,3696]{2,1,0:T(4,128)(2,1)} async-done(((bf16[128,4,3696]{2,1,0:T(4,128)(2,1)}), bf16[128,4,3696]{2,1,0:T(4,128)(2,1)}, u32[]{:S(2)}, u32[]{:S(2)}) %all-to-all-start.1) | async-done | bytes 3784736 | tf_op jit(solution)/shard_map/all_to_all | solution.py:89
  351.3 7.0 %reshape.40 = bf16[512,3696]{1,0:T(8,128)(2,1)} reshape(bf16[128,4,3696]{2,1,0:T(4,128)(2,1)} %all-to-all-done.1) | data formatting | bytes 7569408 | tf_op jit(solution)/shard_map/reshape | solution.py:104
  358.3 5.9 %gather_fusion = bf16[128,3696]{1,0:T(8,128)(2,1)} fusion(bf16[512,3696]{1,0:T(8,128)(2,1)} %reshape.40, s32[1024]{0:T(1024)S(1)} %pad_clamp_fusion), kind=kCustom, calls=%fused_computation | custom fusion | bytes 1892864 | tf_op jit(solution)/shard_map/gather | solution.py:109
  364.2 29.1 %reduce-scatter.4.cloned.1.call-done = bf16[128,7392]{1,0:T(8,128)(2,1)} async-done(((bf16[2048,7392]{1,0:T(8,128)(2,1)}), bf16[128,7392]{1,0:T(8,128)(2,1)}) %reduce-scatter.4.cloned.1.call-update) | async-done | bytes 1892368 | tf_op jit(solution)/shard_map/reduce_scatter | solution.py:33
  (32 shorter events, 11.3 us)
Async XLA Ops:
  6.5 159.8 %copy-start = (bf16[1,8192,128]{2,1,0:T(8,128)(2,1)S(1)}, bf16[1,8192,128]{2,1,0:T(8,128)(2,1)}, u32[]{:S(2)}) copy-start(bf16[1,8192,128]{2,1,0:T(8,128)(2,1)} %param.10) | copy-start | bytes 6291460
  6.5 31.4 %all-gather.2.cloned.1.call-start = ((), (), s32[]{:S(2)}) async-start(), calls=%async_computation.4 | async-start | bytes 2359296 | tf_op jit(solution)/shard_map/all_gather | solution.py:32
  7.3 386.0 %reduce-scatter.4.cloned.1.call-start = ((), (), s32[]{:S(2)}) async-start(), calls=%async_computation.5 | async-start | bytes 32309248 | tf_op jit(solution)/shard_map/reduce_scatter | solution.py:33
  37.9 13.8 %copy-start.5 = (bf16[512,3696]{0,1:T(8,128)(2,1)S(1)}, bf16[512,3696]{0,1:T(8,128)(2,1)}, u32[]{:S(2)}) copy-start(bf16[512,3696]{0,1:T(8,128)(2,1)} %param.8) | copy-start | bytes 11354116
  37.9 13.8 %copy-start.6 = (bf16[2048,512]{1,0:T(8,128)(2,1)S(1)}, bf16[2048,512]{1,0:T(8,128)(2,1)}, u32[]{:S(2)}) copy-start(bf16[2048,512]{1,0:T(8,128)(2,1)} %all-gather.2.cloned.1.call-done) | copy-start | bytes 6291460
  120.5 0.7 copy-start.3
  120.5 0.7 copy-start.4
  127.9 38.4 %all-to-all-start = ((bf16[128,8,512]{2,1,0:T(8,128)(2,1)}), bf16[128,8,512]{2,1,0:T(8,128)(2,1)S(1)}, u32[]{:S(2)}, u32[]{:S(2)}) async-start(bf16[128,8,512]{2,1,0:T(8,128)(2,1)} %bitcast.48), calls=%async_computation | async-start | bytes 2097152 | tf_op jit(solution)/shard_map/all_to_all | solution.py:57
  175.8 87.8 %all-to-all-start.2 = ((bf16[128,4,3696]{2,1,0:T(4,128)(2,1)}), bf16[128,4,3696]{2,1,0:T(4,128)(2,1)}, u32[]{:S(2)}, u32[]{:S(2)}) async-start(bf16[128,4,3696]{2,1,0:T(4,128)(2,1)} %copy.56), calls=%async_computation.2 | async-start | bytes 7602176 | tf_op jit(solution)/shard_map/all_to_all | solution.py:96
  263.6 87.7 %all-to-all-start.1 = ((bf16[128,4,3696]{2,1,0:T(4,128)(2,1)}), bf16[128,4,3696]{2,1,0:T(4,128)(2,1)}, u32[]{:S(2)}, u32[]{:S(2)}) async-start(bf16[128,4,3696]{2,1,0:T(4,128)(2,1)} %copy.52), calls=%async_computation.1 | async-start | bytes 7602176 | tf_op jit(solution)/shard_map/all_to_all | solution.py:89
  393.3 1.9 copy-start.1
  393.3 2.0 copy-start.2
Sparse Core Ops, SparseCore 0:
  9.1 28.7 all-gather.1
  120.6 272.5 reduce-scatter.3
where the time goes:
time: 406 us; the launch traced here: 404 us
  waiting for transfers between devices  211 us (52%)
  local copies, waits for them, and re-layouts  99.4 us (24%)
  matrix products  31.7 us (8%)
  other arithmetic  27.8 us (7%)
  starting transfers between devices  20.6 us (5%)
  between operations  13.5 us (3%)
    all_to_all x1, waiting for transfers between devices, body(): lax.all_to_all(delta_gate.reshape(devices, CAP, column_count), ('gx', 'gy...  68.3 us
    all_to_all x1, waiting for transfers between devices, body(): lax.all_to_all(delta_up.reshape(devices, CAP, column_count), ('gx', 'gy')...  65.6 us
    unnamed x15, local copies, waits for them, and re-layouts  37.3 us
    all_gather x1, waiting for transfers between devices, body(): gathered = lax.all_gather(tokens, 'gy', axis=0, tiled=True)  30.6 us
    reduce_scatter x1, waiting for transfers between devices, body(): lax.psum_scatter(jnp.concatenate([jnp.dot(gathered, gate_base_weight, pre...  29.1 us
    concatenate x1, other arithmetic, body(): jnp.concatenate([jnp.dot(gathered, gate_base_weight, preferred_element_ty...  21.4 us
    all_to_all x1, waiting for transfers between devices, body(): lax.all_to_all(outgoing.reshape(devices, groups * CAP, tile_width), ('gx'...  17.1 us
    dot_general x1, matrix products, body(): jnp.dot(gathered, up_base_weight, preferred_element_type=jnp.float32)  13.8 us
  transfers between devices with their start and end apart: 5, of which 5 were waited for; matrix products, arithmetic and copies ran while one was open for 18% of the time, Pallas kernels for 0%

commit v1 on v0

--- a/solution.py
+++ b/solution.py
@@ -29,7 +29,19 @@
     column_count = gate_base_weight.shape[1]
     doubled_rank = adapter_down_maps.shape[2]
     adapter_rank_width = doubled_rank // 2
-    gathered = lax.all_gather(tokens, "gy", axis=0, tiled=True)
+    lanes = jax.lax.axis_size("gy")
+    all_blocks = [(to_i, (to_i + 1) % lanes) for to_i in range(lanes)]
+    line_up = [(to_i, (to_i - 1) % lanes) for to_i in range(lanes)]
+    f_next, z = ([tokens], [tokens])
+    for _ in range(lanes // 2):
+        f_next.append(jax.lax.ppermute(f_next[-1], "gy", all_blocks))
+    for _ in range((lanes - 1) // 2):
+        z.append(jax.lax.ppermute(z[-1], "gy", line_up))
+    gathered = jnp.roll(
+        jnp.concatenate([*f_next[::-1], *z[1:]], 0),
+        (jax.lax.axis_index("gy") - lanes // 2) * tokens.shape[0],
+        0,
+    )
     summed = lax.psum_scatter(
         jnp.concatenate(
             [

time: 406 us -> 407 us (level)
  waiting for transfers between devices: 211 us -> 192 us
  starting transfers between devices: 20.6 us -> 38.8 us
  local copies, waits for them, and re-layouts: 99.4 us -> 104 us
    all_gather x1 -> x0, waiting for transfers between devices: 30.6 us -> none  [body(): gathered = lax.all_gather(tokens, 'gy', axis=0, tiled=True)]
    ppermute x0 -> x7, starting transfers between devices: none -> 12.5 us  [the longest x4 10.1 us: body(): f_next.append(jax.lax.ppermute(f_next[-1], 'gy', all_blocks))]
    ppermute x0 -> x7, waiting for transfers between devices: none -> 11.8 us  [the longest x4 10.3 us: body(): f_next.append(jax.lax.ppermute(f_next[-1], 'gy', all_blocks))]
    all_to_all x1, starting transfers between devices: 8.15 us -> 13.2 us  [body(): lax.all_to_all(outgoing.reshape(devices, groups * CAP, tile_width), ('gx'...]
    unnamed x15 -> x32, local copies, waits for them, and re-layouts: 37.3 us -> 42.3 us
  transfers between devices with their start and end apart: 5 -> 11, of which waited for: 5 -> 11; matrix products, arithmetic and copies ran while one was open for 18% -> 18% of each run, Pallas kernels for 0% -> 0%
where the time goes in v1:
time: 407 us; the launch traced here: 404 us
  waiting for transfers between devices  192 us (47%)
  local copies, waits for them, and re-layouts  104 us (26%)
  starting transfers between devices  38.8 us (10%)
  matrix products  28.6 us (7%)
  other arithmetic  27.8 us (7%)
  between operations  13.6 us (3%)
    all_to_all x1, waiting for transfers between devices, body(): lax.all_to_all(delta_up.reshape(devices, CAP, column_count), ('gx', 'gy')...  68.8 us
    all_to_all x1, waiting for transfers between devices, body(): lax.all_to_all(delta_gate.reshape(devices, CAP, column_count), ('gx', 'gy...  65 us
    unnamed x32, local copies, waits for them, and re-layouts  42.3 us
    reduce_scatter x1, waiting for transfers between devices, body(): lax.psum_scatter(jnp.concatenate([jnp.dot(gathered, gate_base_weight, pre...  29.1 us
    concatenate x1, other arithmetic, body(): jnp.concatenate([jnp.dot(gathered, gate_base_weight, preferred_element_ty...  21.4 us
    all_to_all x1, waiting for transfers between devices, body(): lax.all_to_all(outgoing.reshape(devices, groups * CAP, tile_width), ('gx'...  17.2 us
    all_to_all x1, starting transfers between devices, body(): lax.all_to_all(outgoing.reshape(devices, groups * CAP, tile_width), ('gx'...  13.2 us
    dot_general x1, matrix products, body(): jnp.dot(gathered, gate_base_weight, preferred_element_type=jnp.float32)  10.8 us
  transfers between devices with their start and end apart: 11, of which 11 were waited for; matrix products, arithmetic and copies ran while one was open for 18% of the time, Pallas kernels for 0%

profile of v1, /device:TPU:1, one launch (start us, length us, event | category | flops | bytes accessed | tf_op | source)
XLA Modules:
  0.0 404.5 jit_solution(10574524386551290324)
XLA Ops:
  9.2 3.6 collective-permute-done
  15.2 3.3 collective-permute-done.1
  36.1 10.8 %convolution_convert_fusion.1 = bf16[2048,3696]{0,1:T(8,128)(2,1)} fusion(bf16[512,3696]{0,1:T(8,128)(2,1)S(1)} %copy-done.6, bf16[4096,512]{1,0:T(8,128)(2,1)S(1)} %constant_dynamic-update-slice_fusion, s32[]{:T(128)S(6)} %select_n.38), kind=kOutput, calls=%fused_computation.5 | convolution fusion | flops 7758643200 | bytes 21020676 | tf_op jit(solution)/shard_map/dot_general | solution.py:48
  46.9 10.8 %convolution_convert_fusion = bf16[2048,3696]{0,1:T(8,128)(2,1)} fusion(bf16[512,3696]{0,1:T(8,128)(2,1)S(1)} %copy-done.7, bf16[4096,512]{1,0:T(8,128)(2,1)S(1)} %constant_dynamic-update-slice_fusion, s32[]{:T(128)S(6)} %select_n.38), kind=kOutput, calls=%fused_computation.4 | convolution fusion | flops 7758643200 | bytes 21020676 | tf_op jit(solution)/shard_map/dot_general | solution.py:49
  57.7 21.4 %pad_maximum_fusion = bf16[2048,7392]{0,1:T(8,128)(2,1)} fusion(bf16[2048,3696]{0,1:T(8,128)(2,1)} %convolution_convert_fusion, bf16[2048,3696]{0,1:T(8,128)(2,1)} %convolution_convert_fusion.1), kind=kLoop, calls=%fused_computation.3 | loop fusion | flops 60555264 | bytes 60555264 | tf_op jit(solution)/shard_map/concatenate | solution.py:46
  79.2 36.4 %copy.60 = bf16[2048,7392]{1,0:T(8,128)(2,1)} copy(bf16[2048,7392]{0,1:T(8,128)(2,1)} %pad_maximum_fusion) | data formatting | bytes 60555264
  122.6 13.2 %all-to-all-start = ((bf16[128,8,512]{2,1,0:T(8,128)(2,1)}), bf16[128,8,512]{2,1,0:T(8,128)(2,1)S(1)}, u32[]{:S(2)}, u32[]{:S(2)}) async-start(bf16[128,8,512]{2,1,0:T(8,128)(2,1)} %bitcast.46), calls=%async_computation | async-start | bytes 2097152 | tf_op jit(solution)/shard_map/all_to_all | solution.py:69
  135.8 5.5 %fusion.23 = (bf16[1,64,29568]{2,1,0:T(8,128)(2,1)}, bf16[1,64,29568]{2,1,0:T(8,128)(2,1)}) fusion(bf16[1,128,29568]{2,1,0:T(8,128)(2,1)} %param.11), kind=kLoop, calls=%fused_computation.64 | loop fusion | bytes 15138816 | tf_op jit(solution)/shard_map/slice | solution.py:82
  141.3 7.5 %reshape_squeeze.10 = bf16[64,8,3696]{2,1,0:T(8,128)(2,1)} reshape(bf16[1,64,29568]{2,1,0:T(8,128)(2,1)} %get-tuple-element.5) | data formatting | bytes 7569408 | tf_op jit(solution)/shard_map/reshape;squeeze | solution.py:82
  148.8 17.2 %all-to-all-done = bf16[128,8,512]{2,1,0:T(8,128)(2,1)S(1)} async-done(((bf16[128,8,512]{2,1,0:T(8,128)(2,1)}), bf16[128,8,512]{2,1,0:T(8,128)(2,1)S(1)}, u32[]{:S(2)}, u32[]{:S(2)}) %all-to-all-start) | async-done | bytes 1048608 | tf_op jit(solution)/shard_map/all_to_all | solution.py:69
  166.6 3.2 fusion
  170.5 4.9 %copy.52 = bf16[128,4,3696]{2,1,0:T(4,128)(2,1)} copy(bf16[128,4,3696]{2,0,1:T(8,128)(2,1)S(1)} %bitcast.43) | data formatting | bytes 7569408 | tf_op jit(solution)/shard_map/reshape | solution.py:102
  175.4 5.9 %all-to-all-start.1 = ((bf16[128,4,3696]{2,1,0:T(4,128)(2,1)}), bf16[128,4,3696]{2,1,0:T(4,128)(2,1)}, u32[]{:S(2)}, u32[]{:S(2)}) async-start(bf16[128,4,3696]{2,1,0:T(4,128)(2,1)} %copy.52), calls=%async_computation.1 | async-start | bytes 7602176 | tf_op jit(solution)/shard_map/all_to_all | solution.py:101
  181.3 7.6 %reshape_squeeze.11 = bf16[64,8,3696]{2,1,0:T(8,128)(2,1)} reshape(bf16[1,64,29568]{2,1,0:T(8,128)(2,1)} %get-tuple-element.6) | data formatting | bytes 7569408 | tf_op jit(solution)/shard_map/reshape;squeeze | solution.py:85
  188.9 3.2 fusion.1
  192.7 4.8 %copy.56 = bf16[128,4,3696]{2,1,0:T(4,128)(2,1)} copy(bf16[128,4,3696]{2,0,1:T(8,128)(2,1)S(1)} %bitcast.44) | data formatting | bytes 7569408 | tf_op jit(solution)/shard_map/reshape | solution.py:109
  197.5 65.0 %all-to-all-done.1 = bf16[128,4,3696]{2,1,0:T(4,128)(2,1)} async-done(((bf16[128,4,3696]{2,1,0:T(4,128)(2,1)}), bf16[128,4,3696]{2,1,0:T(4,128)(2,1)}, u32[]{:S(2)}, u32[]{:S(2)}) %all-to-all-start.1) | async-done | bytes 3784736 | tf_op jit(solution)/shard_map/all_to_all | solution.py:101
  262.5 7.2 %all-to-all-start.2 = ((bf16[128,4,3696]{2,1,0:T(4,128)(2,1)}), bf16[128,4,3696]{2,1,0:T(4,128)(2,1)}, u32[]{:S(2)}, u32[]{:S(2)}) async-start(bf16[128,4,3696]{2,1,0:T(4,128)(2,1)} %copy.56), calls=%async_computation.2 | async-start | bytes 7602176 | tf_op jit(solution)/shard_map/all_to_all | solution.py:108
  269.8 7.2 %reshape.40 = bf16[512,3696]{1,0:T(8,128)(2,1)} reshape(bf16[128,4,3696]{2,1,0:T(4,128)(2,1)} %all-to-all-done.1) | data formatting | bytes 7569408 | tf_op jit(solution)/shard_map/reshape | solution.py:116
  276.9 5.6 %gather_fusion = bf16[128,3696]{1,0:T(8,128)(2,1)} fusion(bf16[512,3696]{1,0:T(8,128)(2,1)} %reshape.40, s32[1024]{0:T(1024)S(1)} %pad_clamp_fusion), kind=kCustom, calls=%fused_computation | custom fusion | bytes 1892864 | tf_op jit(solution)/shard_map/gather | solution.py:121
  282.5 68.8 %all-to-all-done.2 = bf16[128,4,3696]{2,1,0:T(4,128)(2,1)} async-done(((bf16[128,4,3696]{2,1,0:T(4,128)(2,1)}), bf16[128,4,3696]{2,1,0:T(4,128)(2,1)}, u32[]{:S(2)}, u32[]{:S(2)}) %all-to-all-start.2) | async-done | bytes 3784736 | tf_op jit(solution)/shard_map/all_to_all | solution.py:108
  351.3 7.0 %reshape.42 = bf16[512,3696]{1,0:T(8,128)(2,1)} reshape(bf16[128,4,3696]{2,1,0:T(4,128)(2,1)} %all-to-all-done.2) | data formatting | bytes 7569408 | tf_op jit(solution)/shard_map/reshape | solution.py:117
  358.3 6.0 %gather_fusion.1 = bf16[128,3696]{1,0:T(8,128)(2,1)} fusion(bf16[512,3696]{1,0:T(8,128)(2,1)} %reshape.42, s32[1024]{0:T(1024)S(1)} %pad_clamp_fusion), kind=kCustom, calls=%fused_computation.1 | custom fusion | bytes 1892864 | tf_op jit(solution)/shard_map/gather | solution.py:122
  364.3 29.1 %reduce-scatter.4.cloned.1.call-done = bf16[128,7392]{1,0:T(8,128)(2,1)} async-done(((bf16[2048,7392]{1,0:T(8,128)(2,1)}), bf16[128,7392]{1,0:T(8,128)(2,1)}) %reduce-scatter.4.cloned.1.call-update) | async-done | bytes 1892368 | tf_op jit(solution)/shard_map/reduce_scatter | solution.py:45
  (61 shorter events, 35.7 us)
Async XLA Ops:
  6.5 159.5 %copy-start = (bf16[1,8192,128]{2,1,0:T(8,128)(2,1)S(1)}, bf16[1,8192,128]{2,1,0:T(8,128)(2,1)}, u32[]{:S(2)}) copy-start(bf16[1,8192,128]{2,1,0:T(8,128)(2,1)} %param.10) | copy-start | bytes 6291460
  6.5 29.4 %copy-start.3 = (bf16[256,512]{1,0:T(8,128)(2,1)S(1)}, bf16[256,512]{1,0:T(8,128)(2,1)}, u32[]{:S(2)}) copy-start(bf16[256,512]{1,0:T(8,128)(2,1)} %param.7) | copy-start | bytes 786436
  6.5 386.9 %reduce-scatter.4.cloned.1.call-start = ((), (), s32[]{:S(2)}) async-start(), calls=%async_computation.4 | async-start | bytes 32309248 | tf_op jit(solution)/shard_map/reduce_scatter | solution.py:45
  6.5 6.3 %collective-permute-start = (bf16[256,512]{1,0:T(8,128)(2,1)}, bf16[256,512]{1,0:T(8,128)(2,1)S(1)}, u32[]{:S(2)}, u32[]{:S(2)}) collective-permute-start(bf16[256,512]{1,0:T(8,128)(2,1)} %param.7), channel_id=1, source_target_pairs={{0,1},{1,2},{2,3},{3,4},{4,5},{5,6},{6,7},{7,0},{8,9},{9,10},{10,1... | collective-permute-start | bytes 786440 | tf_op jit(solution)/shard_map/ppermute | solution.py:37
  12.9 5.7 %collective-permute-start.1 = (bf16[256,512]{1,0:T(8,128)(2,1)S(1)}, bf16[256,512]{1,0:T(8,128)(2,1)S(1)}, u32[]{:S(2)}, u32[]{:S(2)}) collective-permute-start(bf16[256,512]{1,0:T(8,128)(2,1)S(1)} %collective-permute-done), channel_id=1, source_target_pairs={{0,1},{1,2},{2,3},{3,4},{4,5},{5,6},{6,7},{7,0},{8,9},{9,10},{10,1... | collective-permute-start | bytes 786440 | tf_op jit(solution)/shard_map/ppermute | solution.py:37
  15.2 6.3 %collective-permute-start.4 = (bf16[256,512]{1,0:T(8,128)(2,1)}, bf16[256,512]{1,0:T(8,128)(2,1)S(1)}, u32[]{:S(2)}, u32[]{:S(2)}) collective-permute-start(bf16[256,512]{1,0:T(8,128)(2,1)} %param.7), channel_id=1, source_target_pairs={{0,7},{1,0},{2,1},{3,2},{4,3},{5,4},{6,5},{7,6},{8,15},{9,8},{10,9... | collective-permute-start | bytes 786440 | tf_op jit(solution)/shard_map/ppermute | solution.py:39
  18.6 5.8 %collective-permute-start.2 = (bf16[256,512]{1,0:T(8,128)(2,1)S(1)}, bf16[256,512]{1,0:T(8,128)(2,1)}, u32[]{:S(2)}, u32[]{:S(2)}) collective-permute-start(bf16[256,512]{1,0:T(8,128)(2,1)S(1)} %collective-permute-done.1), channel_id=1, source_target_pairs={{0,1},{1,2},{2,3},{3,4},{4,5},{5,6},{6,7},{7,0},{8,9},{9,10},{10,1... | collective-permute-start | bytes 786440 | tf_op jit(solution)/shard_map/ppermute | solution.py:37
  21.5 6.2 %collective-permute-start.5 = (bf16[256,512]{1,0:T(8,128)(2,1)S(1)}, bf16[256,512]{1,0:T(8,128)(2,1)S(1)}, u32[]{:S(2)}, u32[]{:S(2)}) collective-permute-start(bf16[256,512]{1,0:T(8,128)(2,1)S(1)} %collective-permute-done.4), channel_id=1, source_target_pairs={{0,7},{1,0},{2,1},{3,2},{4,3},{5,4},{6,5},{7,6},{8,15},{9,8},{10,9... | collective-permute-start | bytes 786440 | tf_op jit(solution)/shard_map/ppermute | solution.py:39
  24.4 6.3 %collective-permute-start.3 = (bf16[256,512]{1,0:T(8,128)(2,1)}, bf16[256,512]{1,0:T(8,128)(2,1)}, u32[]{:S(2)}, u32[]{:S(2)}) collective-permute-start(bf16[256,512]{1,0:T(8,128)(2,1)} %collective-permute-done.2), channel_id=1, source_target_pairs={{0,1},{1,2},{2,3},{3,4},{4,5},{5,6},{6,7},{7,0},{8,9},{9,10},{10,1... | collective-permute-start | bytes 786440 | tf_op jit(solution)/shard_map/ppermute | solution.py:37
  26.9 9.1 %copy-start.6 = (bf16[512,3696]{0,1:T(8,128)(2,1)S(1)}, bf16[512,3696]{0,1:T(8,128)(2,1)}, u32[]{:S(2)}) copy-start(bf16[512,3696]{0,1:T(8,128)(2,1)} %param.8) | copy-start | bytes 11354116
  27.7 6.2 %collective-permute-start.6 = (bf16[256,512]{1,0:T(8,128)(2,1)S(1)}, bf16[256,512]{1,0:T(8,128)(2,1)S(1)}, u32[]{:S(2)}, u32[]{:S(2)}) collective-permute-start(bf16[256,512]{1,0:T(8,128)(2,1)S(1)} %collective-permute-done.5), channel_id=1, source_target_pairs={{0,7},{1,0},{2,1},{3,2},{4,3},{5,4},{6,5},{7,6},{8,15},{9,8},{10,9... | collective-permute-start | bytes 786440 | tf_op jit(solution)/shard_map/ppermute | solution.py:39
  36.1 10.8 %copy-start.7 = (bf16[512,3696]{0,1:T(8,128)(2,1)S(1)}, bf16[512,3696]{0,1:T(8,128)(2,1)}, u32[]{:S(2)}) copy-start(bf16[512,3696]{0,1:T(8,128)(2,1)} %param.9) | copy-start | bytes 11354116
  115.6 0.7 copy-start.4
  115.6 0.7 copy-start.5
  122.6 43.4 %all-to-all-start = ((bf16[128,8,512]{2,1,0:T(8,128)(2,1)}), bf16[128,8,512]{2,1,0:T(8,128)(2,1)S(1)}, u32[]{:S(2)}, u32[]{:S(2)}) async-start(bf16[128,8,512]{2,1,0:T(8,128)(2,1)} %bitcast.46), calls=%async_computation | async-start | bytes 2097152 | tf_op jit(solution)/shard_map/all_to_all | solution.py:69
  175.4 87.1 %all-to-all-start.1 = ((bf16[128,4,3696]{2,1,0:T(4,128)(2,1)}), bf16[128,4,3696]{2,1,0:T(4,128)(2,1)}, u32[]{:S(2)}, u32[]{:S(2)}) async-start(bf16[128,4,3696]{2,1,0:T(4,128)(2,1)} %copy.52), calls=%async_computation.1 | async-start | bytes 7602176 | tf_op jit(solution)/shard_map/all_to_all | solution.py:101
  262.5 88.8 %all-to-all-start.2 = ((bf16[128,4,3696]{2,1,0:T(4,128)(2,1)}), bf16[128,4,3696]{2,1,0:T(4,128)(2,1)}, u32[]{:S(2)}, u32[]{:S(2)}) async-start(bf16[128,4,3696]{2,1,0:T(4,128)(2,1)} %copy.56), calls=%async_computation.2 | async-start | bytes 7602176 | tf_op jit(solution)/shard_map/all_to_all | solution.py:108
  393.4 1.9 copy-start.1
  393.4 2.0 copy-start.2
Sparse Core Ops, SparseCore 0:
  115.7 277.6 reduce-scatter.3
